TPU v7x, 32 devices: a whole 2x2x4 slice. The times are simulated.
32 devices in a mesh: cp: 2 (over y), tp: 4 (over x, core), ep: 4 (over z).
Axes of the slice: x: 2, y: 2, z: 4, core: 2. Of those that a mesh axis runs over, the one named last changes fastest.
Arguments:
- query: bfloat16 [8, 512, 4096], P('ep', 'cp', 'tp'), may hold values from -6 to 6
- keys: bfloat16 [8, 512, 512], P('ep', 'cp', 'tp'), may hold values from -6 to 6
- values: bfloat16 [8, 512, 512], P('ep', 'cp', 'tp'), may hold values from -24 to 24
- segment_ids: int32 [8, 512], P('ep', 'cp'), may hold values from 0 to 3, never falling along the last dimension, each value on 1 to 256 neighbouring positions
- query_norm_gain: float32 [128], replicated, may hold values from 0.25 to 1.75
- key_norm_gain: float32 [128], replicated, may hold values from 0.25 to 1.75
- out_weight: bfloat16 [4096, 2048], P('tp', 'cp'), may hold values from -0.09375 to 0.09375
- residual: bfloat16 [8, 512, 2048], P('ep', 'cp'), may hold values from -3 to 3
- norm_gain: float32 [2048], replicated, may hold values from 0.25 to 1.75
- router_weight: bfloat16 [2048, 16], replicated, may hold values from -0.125 to 0.125
- expert_ids: int32 [8, 512, 8], P('ep', 'cp'), may hold values from 0 to 15, all different within a row; in each aligned block of 64 rows (0 to 63, 64 to 127, ..., all dimensions but the last counted through in order) at most 36 rows name the same one
- expert_gate: bfloat16 [16, 2048, 768], P(('tp', 'ep'), None, 'cp'), may hold values from -0.125 to 0.125
- expert_up: bfloat16 [16, 2048, 768], P(('tp', 'ep'), None, 'cp'), may hold values from -0.125 to 0.125
- expert_down: bfloat16 [16, 2048, 768], P(('tp', 'ep'), None, 'cp'), may hold values from -0.21875 to 0.21875
Outputs:
- layer_out: bfloat16 [8, 512, 2048], P('ep', ('cp', 'tp'))
Inputs may be any that keep to these rules, and one draw needn't show every extreme that they name: `segment_ids`: document numbers never fall along a sequence. `expert_ids`: each token names 8 different experts; in every aligned block of 64 positions of a sequence no expert is named by more than 36 tokens, a bound that some block reaches.
All inputs are finite; a program needn't handle non-finite values.
Results may differ from a plain program's by a relative error of at most 0.007.
Values may be sent and summed in bfloat16 or wider, within the bound.
No kernel may reach another device: no remote copies, remote signals or barrier semaphores. Data moves between devices by JAX's collectives and lax.ppermute only.
A program may use at most 128 MiB of HBM per device.

v0:
```python
import jax
import jax.numpy as jnp
from jax import lax
from jax.sharding import PartitionSpec as P

HEAD_WIDTH = 128


def root_mean_scale(entries, gain):
    mean_sq = jnp.mean(entries * entries, axis=-1, keepdims=True)
    return entries * lax.rsqrt(mean_sq + 1e-06) * gain


def capacity(share, top_count, experts):
    return min(
        share, max(2, share * top_count // experts + max(1, share * top_count // (8 * experts)))
    )


def slot_numbers(ids, experts):
    flat_ids = ids.reshape(-1)
    table = (flat_ids[:, None] == jnp.arange(experts, dtype=jnp.int32)[None, :]).astype(jnp.int32)
    before = jnp.cumsum(table, axis=0) - table
    return jnp.sum(before * table, axis=1).reshape(ids.shape)


def route(state, ids, norm_gain, router_weight):
    normed = root_mean_scale(state, norm_gain).astype(jnp.bfloat16)
    logits = jnp.dot(normed, router_weight, preferred_element_type=jnp.float32)
    experts = router_weight.shape[1]
    picks = ids[:, :, None] == jnp.arange(experts, dtype=jnp.int32)[None, None, :]
    chosen = jnp.sum(jnp.where(picks, logits[:, None, :], jnp.float32(0.0)), axis=-1)
    raised = jnp.exp(chosen)
    return (normed, raised / jnp.sum(raised, axis=-1, keepdims=True))


def expert_rows(received, full_gate, full_up, full_down):
    width = received.shape[-1]
    flat_rows = received.reshape(-1, width)
    gate_act = jnp.dot(flat_rows, full_gate[0], preferred_element_type=jnp.float32)
    up_act = jnp.dot(flat_rows, full_up[0], preferred_element_type=jnp.float32)
    hidden_act = (jax.nn.silu(gate_act) * up_act).astype(jnp.bfloat16)
    served = jnp.einsum(
        "rf,df->rd", hidden_act, full_down[0], preferred_element_type=jnp.float32
    ).astype(jnp.bfloat16)
    return served.reshape(received.shape)


def shards(
    query,
    keys,
    values,
    segment_ids,
    query_norm_gain,
    key_norm_gain,
    out_weight,
    residual,
    norm_gain,
    router_weight,
    expert_ids,
    expert_gate,
    expert_up,
    expert_down,
):
    packs = query.shape[0]
    row_count = query.shape[1]
    head_count = query.shape[2] // HEAD_WIDTH
    width = residual.shape[2]
    experts = router_weight.shape[1]
    top_count = expert_ids.shape[2]
    score_scale = HEAD_WIDTH ** (-0.5)
    query_rows_normed = root_mean_scale(
        query.astype(jnp.float32).reshape(packs, row_count, head_count, HEAD_WIDTH), query_norm_gain
    ).astype(jnp.bfloat16)
    key_rows_normed = root_mean_scale(keys.astype(jnp.float32), key_norm_gain).astype(jnp.bfloat16)
    own_docs = segment_ids.astype(jnp.bfloat16)
    key_piece = lax.all_gather(key_rows_normed, "cp", axis=1, tiled=True)
    value_piece = lax.all_gather(values, "cp", axis=1, tiled=True)
    doc_piece = lax.all_gather(own_docs, "cp", axis=1, tiled=True)
    scores = (
        jnp.einsum(
            "pshd,pnd->phsn", query_rows_normed, key_piece, preferred_element_type=jnp.float32
        )
        * score_scale
    )
    same_doc = own_docs[:, :, None] == doc_piece[:, None, :]
    probs = jnp.where(same_doc[:, None], jnp.exp(scores), jnp.float32(0.0))
    denom = jnp.sum(probs, axis=-1)
    probs_b = probs.astype(jnp.bfloat16)
    summed = jnp.einsum("phsn,pnd->pshd", probs_b, value_piece, preferred_element_type=jnp.float32)
    denom, summed = (denom, summed)
    attn = (
        (summed / jnp.transpose(denom, (0, 2, 1))[:, :, :, None])
        .astype(jnp.bfloat16)
        .reshape(packs * row_count, head_count * HEAD_WIDTH)
    )
    partial_proj = jnp.dot(
        attn,
        lax.all_gather(out_weight, "cp", axis=1, tiled=True),
        preferred_element_type=jnp.float32,
    ).reshape(packs, row_count, width)
    full_gate, full_up, full_down = (
        lax.all_gather(expert_gate, "cp", axis=2, tiled=True),
        lax.all_gather(expert_up, "cp", axis=2, tiled=True),
        lax.all_gather(expert_down, "cp", axis=2, tiled=True),
    )
    share = row_count // lax.axis_size("tp")
    tp_index = lax.axis_index("tp")
    cap = capacity(share, top_count, experts)
    projected = lax.psum_scatter(partial_proj, "tp", scatter_dimension=1, tiled=True)
    first_row = tp_index * share
    state = lax.dynamic_slice_in_dim(residual, first_row, share, 1).astype(jnp.float32) + projected
    local_ids = lax.dynamic_slice_in_dim(expert_ids, first_row, share, 1).reshape(
        packs * share, top_count
    )
    normed, gates = route(state.reshape(packs * share, width), local_ids, norm_gain, router_weight)
    dev_cap = packs * cap
    slots = slot_numbers(local_ids, experts)
    target = (local_ids * dev_cap + slots).reshape(-1)
    sent_rows = jnp.broadcast_to(normed[:, None, :], (packs * share, top_count, width)).reshape(
        -1, width
    )
    buffer = (
        jnp.zeros((experts * dev_cap, width), jnp.bfloat16)
        .at[target]
        .set(sent_rows)
        .reshape(experts, dev_cap, width)
    )
    served = expert_rows(
        lax.all_to_all(buffer, ("tp", "ep"), split_axis=0, concat_axis=0, tiled=True),
        full_gate,
        full_up,
        full_down,
    )
    back = lax.all_to_all(served, ("tp", "ep"), split_axis=0, concat_axis=0, tiled=True)
    picked = back.reshape(experts * dev_cap, width)[target].reshape(packs * share, top_count, width)
    mixture = jnp.sum(gates[:, :, None] * picked.astype(jnp.float32), axis=1)
    layer_out = (state + mixture.reshape(packs, share, width)).astype(jnp.bfloat16)
    return layer_out


def solution(mesh):
    return jax.shard_map(
        shards,
        mesh=mesh,
        in_specs=(
            P("ep", "cp", "tp"),
            P("ep", "cp", "tp"),
            P("ep", "cp", "tp"),
            P("ep", "cp"),
            P(),
            P(),
            P("tp", "cp"),
            P("ep", "cp", None),
            P(),
            P(),
            P("ep", "cp", None),
            P(("tp", "ep"), None, "cp"),
            P(("tp", "ep"), None, "cp"),
            P(("tp", "ep"), None, "cp"),
        ),
        out_specs=P("ep", ("cp", "tp"), None),
        check_vma=False,
    )
```

profile of v0, /device:TPU:0, one launch (start us, length us, event | category | flops | bytes accessed | tf_op | source)
XLA Modules:
  0.0 424.7 jit_solution(739500518917911366)
XLA Ops:
  6.6 0.7 all-gather.5.cloned.1.call-update
  7.3 0.7 convert_element_type.52
  8.0 1.5 copy.74
  9.5 0.6 fusion.18
  10.1 0.1 copy.57
  10.2 0.1 copy.58
  10.4 0.1 copy.60
  10.5 5.2 %all_gather.21 = bf16[2,512]{1,0:T(2,128)(2,1)S(1)} all-gather(bf16[2,256]{1,0:T(2,128)(2,1)S(1)} %convert_element_type.52), channel_id=1, replica_groups=mesh['cp'=2,'tp'=4,'ep'=4] {'cp'}, dimensions={1}, use_global_device_ids=true | all-gather | bytes 3072 | tf_op jit(solution)/shard_map/all_gather | solution.py:79
  15.7 0.1 fusion.29
  15.9 0.1 fusion.31
  16.0 5.7 %all_gather.22 = bf16[2,512,128]{2,1,0:T(8,128)(2,1)S(1)} all-gather(bf16[2,256,128]{2,1,0:T(8,128)(2,1)S(1)} %fusion.31), channel_id=1, replica_groups=mesh['cp'=2,'tp'=4,'ep'=4] {'cp'}, dimensions={1}, use_global_device_ids=true | all-gather | bytes 393216 | tf_op jit(solution)/shard_map/all_gather | solution.py:77
  21.6 8.7 %all_gather.23 = bf16[2,512,128]{1,2,0:T(8,128)(2,1)S(1)} all-gather(bf16[2,256,128]{1,2,0:T(8,128)(2,1)S(1)} %copy.60), channel_id=1, replica_groups=mesh['cp'=2,'tp'=4,'ep'=4] {'cp'}, dimensions={1}, use_global_device_ids=true | all-gather | bytes 393216 | tf_op jit(solution)/shard_map/all_gather | solution.py:78
  30.3 0.2 broadcast_compare_fusion
  30.6 0.7 fusion.20
  31.3 2.2 fusion.1
  33.5 1.7 fusion.21
  35.2 35.5 %all-gather.5.cloned.1.call-done = bf16[1024,2048]{1,0:T(8,128)(2,1)} async-done(((bf16[1024,1024]{1,0:T(8,128)(2,1)}), bf16[1024,2048]{1,0:T(8,128)(2,1)}) %all-gather.5.cloned.1.call-update) | async-done | bytes 4194320 | tf_op jit(solution)/shard_map/all_gather | solution.py:99
  70.7 6.5 %fusion.7 = f32[2,256,2048]{2,1,0:T(8,128)} fusion(bf16[2,256,1024]{1,2,0:T(8,128)(2,1)S(1)} %bitcast.104, bf16[1024,2048]{1,0:T(8,128)(2,1)} %all-gather.5.cloned.1.call-done), kind=kOutput, calls=%fused_computation.11 | convolution fusion | flops 2147483648 | bytes 9437184 | tf_op jit(solution)/shard_map/dot_general | solution.py:97
  77.2 0.7 copy-done.4
  78.0 0.1 copy.66
  78.1 0.1 eq.68
  78.2 0.1 eq.64
  78.3 4.5 %reduce-window.6 = s32[16,8,128]{2,1,0:T(8,128)S(1)} reduce-window(s32[16,8,128]{2,1,0:T(8,128)S(1)} %fusion.37, s32[]{:T(128)} %constant.14.clone.1), window={size=1x1x128 pad=0_0x0_0x127_0}, to_apply=%region_7.8 | reduce-window | flops 2080768 | bytes 131076 | tf_op jit(solution)/shard_map/reduce-window
  82.9 0.1 copy.68
  83.1 0.1 copy.65
  83.2 0.1 mul.132
  83.5 39.1 %reduce-scatter.2.cloned.1.call-done = f32[2,64,2048]{2,1,0:T(8,128)} async-done(((f32[2,256,2048]{2,1,0:T(8,128)}), f32[2,64,2048]{2,1,0:T(8,128)}) %reduce-scatter.2.cloned.1.call-update) | async-done | bytes 1048592 | tf_op jit(solution)/shard_map/reduce_scatter | solution.py:110
  122.6 1.6 multiply_reduce_fusion
  124.2 0.1 rsqrt.30
  124.3 0.2 fusion.26
  124.5 9.4 %scatter_custom_fusion = bf16[1152,2048]{1,0:T(8,128)(2,1)} fusion(s32[1024]{0:T(1024)S(1)} %bitcast.109, bf16[]{:T(256)} %constant.37.clone.1, bf16[128,2048]{1,0:T(8,128)(2,1)S(1)} %fusion.26), kind=kCustom, calls=%fused_computation.9 | custom fusion | bytes 5242882 | tf_op jit(solution)/shard_map/scatter | solution.py:126
  133.8 4.8 %all-to-all-start = ((bf16[16,72,2048]{2,1,0:T(8,128)(2,1)}), bf16[16,72,2048]{2,1,0:T(8,128)(2,1)}, u32[]{:S(2)}, u32[]{:S(2)}) async-start(bf16[16,72,2048]{2,1,0:T(8,128)(2,1)} %bitcast.101), calls=%async_computation.1 | async-start | bytes 9437184 | tf_op jit(solution)/shard_map/all_to_all | solution.py:130
  138.7 0.7 all-gather.7.cloned.1.call-update
  139.4 0.5 all-gather.9.cloned.1.call-update
  140.0 0.5 all-gather.11.cloned.1.call-update
  140.5 46.8 %all-gather.7.cloned.1.call-done = bf16[1,2048,768]{2,1,0:T(8,128)(2,1)} async-done(((bf16[1,2048,384]{2,1,0:T(8,128)(2,1)}), bf16[1,2048,768]{2,1,0:T(8,128)(2,1)}) %all-gather.7.cloned.1.call-update) | async-done | bytes 3145744 | tf_op jit(solution)/shard_map/all_gather | solution.py:103
  187.3 57.0 %all-to-all-done = bf16[16,72,2048]{2,1,0:T(8,128)(2,1)} async-done(((bf16[16,72,2048]{2,1,0:T(8,128)(2,1)}), bf16[16,72,2048]{2,1,0:T(8,128)(2,1)}, u32[]{:S(2)}, u32[]{:S(2)}) %all-to-all-start) | async-done | bytes 4718624 | tf_op jit(solution)/shard_map/all_to_all | solution.py:130
  244.3 9.4 %fusion.15 = f32[1152,768]{1,0:T(8,128)} fusion(bf16[1152,2048]{1,0:T(8,128)(2,1)} %bitcast.16, bf16[1,2048,768]{2,1,0:T(8,128)(2,1)} %all-gather.7.cloned.1.call-done), kind=kOutput, calls=%fused_computation.20 | convolution fusion | flops 3623878656 | bytes 11403264 | tf_op jit(solution)/shard_map/dot_general | solution.py:40
  253.7 8.5 %fusion.12 = bf16[1152,768]{1,0:T(8,128)(2,1)S(1)} fusion(bf16[1152,2048]{1,0:T(8,128)(2,1)} %bitcast.16, f32[1152,768]{1,0:T(8,128)} %fusion.15, bf16[1,2048,768]{2,1,0:T(8,128)(2,1)} %all-gather.9.cloned.1.call-done), kind=kOutput, calls=%fused_computation.17 | convolution fusion | flops 3629187072 | bytes 13172736 | tf_op jit(solution)/shard_map/dot_general | solution.py:41
  262.2 18.0 %all-gather.11.cloned.1.call-done = bf16[1,2048,768]{2,1,0:T(8,128)(2,1)} async-done(((bf16[1,2048,384]{2,1,0:T(8,128)(2,1)}), bf16[1,2048,768]{2,1,0:T(8,128)(2,1)}) %all-gather.11.cloned.1.call-update) | async-done | bytes 3145744 | tf_op jit(solution)/shard_map/all_gather | solution.py:105
  280.1 7.4 %convolution_convert_fusion = bf16[1152,2048]{1,0:T(8,128)(2,1)} fusion(bf16[1152,768]{1,0:T(8,128)(2,1)S(1)} %fusion.12, bf16[1,2048,768]{2,1,0:T(8,128)(2,1)} %all-gather.11.cloned.1.call-done), kind=kOutput, calls=%fused_computation.5 | convolution fusion | flops 3626237952 | bytes 9633792 | tf_op jit(solution)/shard_map/rf,df->rd/dot_general | solution.py:43
  287.6 5.7 %all-to-all-start.1 = ((bf16[16,72,2048]{2,1,0:T(8,128)(2,1)}), bf16[16,72,2048]{2,1,0:T(8,128)(2,1)}, u32[]{:S(2)}, u32[]{:S(2)}) async-start(bf16[16,72,2048]{2,1,0:T(8,128)(2,1)} %bitcast.102), calls=%async_computation.2 | async-start | bytes 9437184 | tf_op jit(solution)/shard_map/all_to_all | solution.py:135
  293.3 0.2 fusion.40
  293.7 0.1 copy.64
  293.8 105.2 %all-to-all-done.1 = bf16[16,72,2048]{2,1,0:T(8,128)(2,1)} async-done(((bf16[16,72,2048]{2,1,0:T(8,128)(2,1)}), bf16[16,72,2048]{2,1,0:T(8,128)(2,1)}, u32[]{:S(2)}, u32[]{:S(2)}) %all-to-all-start.1) | async-done | bytes 4718624 | tf_op jit(solution)/shard_map/all_to_all | solution.py:135
  398.9 11.8 %gather_fusion = bf16[1024,2048]{1,0:T(8,128)(2,1)} fusion(bf16[1152,2048]{1,0:T(8,128)(2,1)} %bitcast.21, s32[1024]{0:T(1024)S(1)} %broadcast_clamp_fusion), kind=kCustom, calls=%fused_computation | custom fusion | bytes 8392704 | tf_op jit(solution)/shard_map/gather | solution.py:136
  410.7 6.5 %fusion = f32[128,2048]{1,0:T(8,128)S(1)} fusion(bf16[1024,2048]{1,0:T(8,128)(2,1)} %gather_fusion, f32[128,8]{1,0:T(8,128)S(1)} %copy.64), kind=kLoop, calls=%fused_computation.3 | loop fusion | flops 6029312 | bytes 5246976 | tf_op jit(solution)/shard_map/reduce_sum | solution.py:137
  417.3 0.9 add_convert_fusion
  (38 shorter events, 0.8 us)
Async XLA Ops:
  6.5 286.8 %copy-start = (bf16[2048,16]{0,1:T(8,128)(2,1)S(1)}, bf16[2048,16]{0,1:T(8,128)(2,1)}, u32[]{:S(2)}) copy-start(bf16[2048,16]{0,1:T(8,128)(2,1)} %param.23) | copy-start | bytes 196612
  6.5 3.8 copy-start.2
  6.5 9.1 %copy-start.1 = (bf16[2,256,128]{2,1,0:T(8,128)(2,1)S(1)}, bf16[2,256,128]{2,1,0:T(8,128)(2,1)}, u32[]{:S(2)}) copy-start(bf16[2,256,128]{2,1,0:T(8,128)(2,1)} %param.15) | copy-start | bytes 393220
  6.5 9.3 %copy-start.5 = (f32[128]{0:T(128)S(1)}, f32[128]{0:T(128)}, u32[]{:S(2)}) copy-start(f32[128]{0:T(128)} %param.19) | copy-start | bytes 1540
  6.5 64.2 %all-gather.5.cloned.1.call-start = ((), (), s32[]{:S(2)}) async-start(), calls=%async_computation.3 | async-start | bytes 6291456 | tf_op jit(solution)/shard_map/all_gather | solution.py:99
  7.3 23.3 %copy-start.6 = (f32[128]{0:T(128)S(1)}, f32[128]{0:T(128)}, u32[]{:S(2)}) copy-start(f32[128]{0:T(128)} %param.18) | copy-start | bytes 1540
  7.3 115.3 %reduce-scatter.2.cloned.1.call-start = ((), (), s32[]{:S(2)}) async-start(), calls=%async_computation.4 | async-start | bytes 5242880 | tf_op jit(solution)/shard_map/reduce_scatter | solution.py:110
  77.2 0.7 copy-start.4
  77.2 47.1 %copy-start.3 = (f32[2048]{0:T(1024)S(1)}, f32[2048]{0:T(1024)}, u32[]{:S(2)}) copy-start(f32[2048]{0:T(1024)} %param.22) | copy-start | bytes 24580
  133.8 110.5 %all-to-all-start = ((bf16[16,72,2048]{2,1,0:T(8,128)(2,1)}), bf16[16,72,2048]{2,1,0:T(8,128)(2,1)}, u32[]{:S(2)}, u32[]{:S(2)}) async-start(bf16[16,72,2048]{2,1,0:T(8,128)(2,1)} %bitcast.101), calls=%async_computation.1 | async-start | bytes 9437184 | tf_op jit(solution)/shard_map/all_to_all | solution.py:130
  138.6 48.7 %all-gather.7.cloned.1.call-start = ((), (), s32[]{:S(2)}) async-start(), calls=%async_computation.5 | async-start | bytes 4718592 | tf_op jit(solution)/shard_map/all_gather | solution.py:103
  139.3 114.3 %all-gather.9.cloned.1.call-start = ((), (), s32[]{:S(2)}) async-start(), calls=%async_computation.6 | async-start | bytes 4718592 | tf_op jit(solution)/shard_map/all_gather | solution.py:104
  139.9 140.2 %all-gather.11.cloned.1.call-start = ((), (), s32[]{:S(2)}) async-start(), calls=%async_computation.7 | async-start | bytes 4718592 | tf_op jit(solution)/shard_map/all_gather | solution.py:105
  287.6 111.3 %all-to-all-start.1 = ((bf16[16,72,2048]{2,1,0:T(8,128)(2,1)}), bf16[16,72,2048]{2,1,0:T(8,128)(2,1)}, u32[]{:S(2)}, u32[]{:S(2)}) async-start(bf16[16,72,2048]{2,1,0:T(8,128)(2,1)} %bitcast.102), calls=%async_computation.2 | async-start | bytes 9437184 | tf_op jit(solution)/shard_map/all_to_all | solution.py:135
Sparse Core Ops, SparseCore 0:
  8.9 61.7 all-gather.4
  77.4 45.2 reduce-scatter.1
  141.1 46.1 all-gather.6
  188.7 44.9 all-gather.8
  235.2 44.9 all-gather.10
where the time goes:
time: 425 us
  waiting for transfers between devices  304 us (72%)
  matrix products  35.9 us (8%)
  local copies, waits for them, and re-layouts  24.7 us (6%)
  blocking collectives  19.5 us (5%)
  other arithmetic  16.6 us (4%)
  between operations  13.4 us (3%)
  starting transfers between devices  10.6 us (2%)
    all_to_all x1, waiting for transfers between devices, shards(): lax.all_to_all(served, ('tp', 'ep'), split_axis=0, concat_axis=0, tiled=T...  105 us
    all_to_all x1, waiting for transfers between devices, shards(): lax.all_to_all(buffer, ('tp', 'ep'), split_axis=0, concat_axis=0, tiled=T...  57 us
    all_gather x1, waiting for transfers between devices, shards(): lax.all_gather(expert_gate, 'cp', axis=2, tiled=True)  46.8 us
    reduce_scatter x1, waiting for transfers between devices, shards(): lax.psum_scatter(partial_proj, 'tp', scatter_dimension=1, tiled=True)  39.1 us
    all_gather x1, waiting for transfers between devices, shards(): lax.all_gather(out_weight, 'cp', axis=1, tiled=True)  35.5 us
    all_gather x1, waiting for transfers between devices, shards(): lax.all_gather(expert_down, 'cp', axis=2, tiled=True)  18 us
    gather x1, local copies, waits for them, and re-layouts, shards(): back.reshape(experts * dev_cap, width)[target]  11.8 us
    dot_general x1, matrix products, expert_rows(): jnp.dot(flat_rows, full_gate[0], preferred_element_type=jnp.float32)  9.4 us
  transfers between devices with their start and end apart: 7, of which 6 were waited for; matrix products, arithmetic and copies ran while one was open for 8% of the time, Pallas kernels for 0%

commit v1 on v0

--- a/solution.py
+++ b/solution.py
@@ -4,6 +4,18 @@
 from jax.sharding import PartitionSpec as P
 
 HEAD_WIDTH = 128
+
+
+def collect(shard, axis, dim):
+    ways, here = (lax.axis_size(axis), lax.axis_index(axis))
+    grown, reach = (shard, 1)
+    while reach < ways:
+        theirs = lax.ppermute(grown, axis, [(d, d ^ reach) for d in range(ways)])
+        mine_first = jnp.concatenate([grown, theirs], axis=dim)
+        theirs_first = jnp.concatenate([theirs, grown], axis=dim)
+        grown = jnp.where(here & reach == 0, mine_first, theirs_first)
+        reach = 2 * reach
+    return grown
 
 
 def root_mean_scale(entries, gain):
@@ -102,7 +114,7 @@
     full_gate, full_up, full_down = (
         lax.all_gather(expert_gate, "cp", axis=2, tiled=True),
         lax.all_gather(expert_up, "cp", axis=2, tiled=True),
-        lax.all_gather(expert_down, "cp", axis=2, tiled=True),
+        collect(expert_down, "cp", 2),
     )
     share = row_count // lax.axis_size("tp")
     tp_index = lax.axis_index("tp")

time: 425 us -> 412 us (0.969)
  waiting for transfers between devices: 304 us -> 289 us
    all_to_all x1, waiting for transfers between devices: 57 us -> 33.7 us  [shards(): lax.all_to_all(buffer, ('tp', 'ep'), split_axis=0, concat_axis=0, tiled=T...]
    all_gather x1, waiting for transfers between devices: 46.8 us -> 69.1 us  [shards(): lax.all_gather(expert_gate, 'cp', axis=2, tiled=True)]
    all_gather x1 -> x0, waiting for transfers between devices: 18 us -> none  [shards(): lax.all_gather(expert_down, 'cp', axis=2, tiled=True)]
    all_gather x1, waiting for transfers between devices: 0.01 us -> 4.88 us  [shards(): lax.all_gather(expert_up, 'cp', axis=2, tiled=True)]
where the time goes in v1:
time: 412 us
  waiting for transfers between devices  289 us (70%)
  matrix products  36.1 us (9%)
  local copies, waits for them, and re-layouts  24.7 us (6%)
  blocking collectives  19.5 us (5%)
  other arithmetic  16.6 us (4%)
  between operations  13.4 us (3%)
  starting transfers between devices  12.3 us (3%)
    all_to_all x1, waiting for transfers between devices, shards(): lax.all_to_all(served, ('tp', 'ep'), split_axis=0, concat_axis=0, tiled=T...  105 us
    all_gather x1, waiting for transfers between devices, shards(): lax.all_gather(expert_gate, 'cp', axis=2, tiled=True)  69.1 us
    reduce_scatter x1, waiting for transfers between devices, shards(): lax.psum_scatter(partial_proj, 'tp', scatter_dimension=1, tiled=True)  39.1 us
    all_gather x1, waiting for transfers between devices, shards(): lax.all_gather(out_weight, 'cp', axis=1, tiled=True)  35.5 us
    all_to_all x1, waiting for transfers between devices, shards(): lax.all_to_all(buffer, ('tp', 'ep'), split_axis=0, concat_axis=0, tiled=T...  33.7 us
    gather x1, local copies, waits for them, and re-layouts, shards(): back.reshape(experts * dev_cap, width)[target]  11.8 us
    scatter x1, local copies, waits for them, and re-layouts, shards(): buffer = jnp.zeros((experts * dev_cap, width), jnp.bfloat16).at[target].s...  9.36 us
    dot_general x1, matrix products, expert_rows(): jnp.dot(flat_rows, full_gate[0], preferred_element_type=jnp.float32)  8.93 us
  transfers between devices with their start and end apart: 7, of which 6 were waited for; matrix products, arithmetic and copies ran while one was open for 8% of the time, Pallas kernels for 0%

profile of v1, /device:TPU:0, one launch (start us, length us, event | category | flops | bytes accessed | tf_op | source)
XLA Modules:
  0.0 411.9 jit_solution(6676020861126850537)
XLA Ops:
  6.6 0.7 all-gather.4.cloned.1.call-update
  7.3 0.7 convert_element_type.52
  8.0 1.5 copy.74
  9.5 0.6 fusion.23
  10.1 0.1 copy.57
  10.2 0.1 copy.58
  10.4 0.1 copy.60
  10.5 5.2 %all_gather.18 = bf16[2,512]{1,0:T(2,128)(2,1)S(1)} all-gather(bf16[2,256]{1,0:T(2,128)(2,1)S(1)} %convert_element_type.52), channel_id=1, replica_groups=mesh['cp'=2,'tp'=4,'ep'=4] {'cp'}, dimensions={1}, use_global_device_ids=true | all-gather | bytes 3072 | tf_op jit(solution)/shard_map/all_gather | solution.py:91
  15.7 0.1 fusion.34
  15.9 0.1 fusion.36
  16.0 5.7 %all_gather.19 = bf16[2,512,128]{2,1,0:T(8,128)(2,1)S(1)} all-gather(bf16[2,256,128]{2,1,0:T(8,128)(2,1)S(1)} %fusion.36), channel_id=1, replica_groups=mesh['cp'=2,'tp'=4,'ep'=4] {'cp'}, dimensions={1}, use_global_device_ids=true | all-gather | bytes 393216 | tf_op jit(solution)/shard_map/all_gather | solution.py:89
  21.6 8.7 %all_gather.20 = bf16[2,512,128]{1,2,0:T(8,128)(2,1)S(1)} all-gather(bf16[2,256,128]{1,2,0:T(8,128)(2,1)S(1)} %copy.60), channel_id=1, replica_groups=mesh['cp'=2,'tp'=4,'ep'=4] {'cp'}, dimensions={1}, use_global_device_ids=true | all-gather | bytes 393216 | tf_op jit(solution)/shard_map/all_gather | solution.py:90
  30.3 0.2 broadcast_compare_fusion
  30.6 0.7 fusion.25
  31.3 2.2 fusion.1
  33.5 1.7 fusion.26
  35.2 35.5 %all-gather.4.cloned.1.call-done = bf16[1024,2048]{1,0:T(8,128)(2,1)} async-done(((bf16[1024,1024]{1,0:T(8,128)(2,1)}), bf16[1024,2048]{1,0:T(8,128)(2,1)}) %all-gather.4.cloned.1.call-update) | async-done | bytes 4194320 | tf_op jit(solution)/shard_map/all_gather | solution.py:111
  70.7 6.5 %fusion.7 = f32[2,256,2048]{2,1,0:T(8,128)} fusion(bf16[2,256,1024]{1,2,0:T(8,128)(2,1)S(1)} %bitcast.103, bf16[1024,2048]{1,0:T(8,128)(2,1)} %all-gather.4.cloned.1.call-done), kind=kOutput, calls=%fused_computation.11 | convolution fusion | flops 2147483648 | bytes 9437184 | tf_op jit(solution)/shard_map/dot_general | solution.py:109
  77.2 0.7 copy-done.4
  78.0 0.1 copy.66
  78.1 0.1 eq.71
  78.2 0.1 eq.67
  78.3 4.5 %reduce-window.6 = s32[16,8,128]{2,1,0:T(8,128)S(1)} reduce-window(s32[16,8,128]{2,1,0:T(8,128)S(1)} %fusion.42, s32[]{:T(128)} %constant.17.clone.1), window={size=1x1x128 pad=0_0x0_0x127_0}, to_apply=%region_7.8 | reduce-window | flops 2080768 | bytes 131076 | tf_op jit(solution)/shard_map/reduce-window
  82.9 0.1 copy.68
  83.1 0.1 copy.65
  83.2 0.1 mul.132
  83.5 39.1 %reduce-scatter.2.cloned.1.call-done = f32[2,64,2048]{2,1,0:T(8,128)} async-done(((f32[2,256,2048]{2,1,0:T(8,128)}), f32[2,64,2048]{2,1,0:T(8,128)}) %reduce-scatter.2.cloned.1.call-update) | async-done | bytes 1048592 | tf_op jit(solution)/shard_map/reduce_scatter | solution.py:122
  122.6 1.6 multiply_reduce_fusion
  124.2 0.1 rsqrt.30
  124.3 0.2 fusion.31
  124.5 9.4 %scatter_custom_fusion = bf16[1152,2048]{1,0:T(8,128)(2,1)} fusion(s32[1024]{0:T(1024)S(1)} %bitcast.108, bf16[]{:T(256)} %constant.42.clone.1, bf16[128,2048]{1,0:T(8,128)(2,1)S(1)} %fusion.31), kind=kCustom, calls=%fused_computation.9 | custom fusion | bytes 5242882 | tf_op jit(solution)/shard_map/scatter | solution.py:138
  133.8 4.9 %all-to-all-start = ((bf16[16,72,2048]{2,1,0:T(8,128)(2,1)}), bf16[16,72,2048]{2,1,0:T(8,128)(2,1)}, u32[]{:S(2)}, u32[]{:S(2)}) async-start(bf16[16,72,2048]{2,1,0:T(8,128)(2,1)} %bitcast.100), calls=%async_computation.1 | async-start | bytes 9437184 | tf_op jit(solution)/shard_map/all_to_all | solution.py:142
  138.8 0.7 all-gather.6.cloned.1.call-update
  139.5 0.5 all-gather.8.cloned.1.call-update
  140.0 1.6 collective-permute-start
  141.6 69.1 %all-gather.6.cloned.1.call-done = bf16[1,2048,768]{2,1,0:T(8,128)(2,1)} async-done(((bf16[1,2048,384]{2,1,0:T(8,128)(2,1)}), bf16[1,2048,768]{2,1,0:T(8,128)(2,1)}) %all-gather.6.cloned.1.call-update) | async-done | bytes 3145744 | tf_op jit(solution)/shard_map/all_gather | solution.py:115
  210.7 33.7 %all-to-all-done = bf16[16,72,2048]{2,1,0:T(8,128)(2,1)} async-done(((bf16[16,72,2048]{2,1,0:T(8,128)(2,1)}), bf16[16,72,2048]{2,1,0:T(8,128)(2,1)}, u32[]{:S(2)}, u32[]{:S(2)}) %all-to-all-start) | async-done | bytes 4718624 | tf_op jit(solution)/shard_map/all_to_all | solution.py:142
  244.4 8.9 %fusion.19 = f32[1152,768]{1,0:T(8,128)} fusion(bf16[1152,2048]{1,0:T(8,128)(2,1)} %bitcast.16, bf16[1,2048,768]{2,1,0:T(8,128)(2,1)} %all-gather.6.cloned.1.call-done), kind=kOutput, calls=%fused_computation.25 | convolution fusion | flops 3623878656 | bytes 11403264 | tf_op jit(solution)/shard_map/dot_general | solution.py:52
  253.3 4.9 %all-gather.8.cloned.1.call-done = bf16[1,2048,768]{2,1,0:T(8,128)(2,1)} async-done(((bf16[1,2048,384]{2,1,0:T(8,128)(2,1)}), bf16[1,2048,768]{2,1,0:T(8,128)(2,1)}) %all-gather.8.cloned.1.call-update) | async-done | bytes 3145744 | tf_op jit(solution)/shard_map/all_gather | solution.py:116
  258.2 8.5 %fusion.12 = bf16[1152,768]{1,0:T(8,128)(2,1)S(1)} fusion(bf16[1152,2048]{1,0:T(8,128)(2,1)} %bitcast.16, f32[1152,768]{1,0:T(8,128)} %fusion.19, bf16[1,2048,768]{2,1,0:T(8,128)(2,1)} %all-gather.8.cloned.1.call-done), kind=kOutput, calls=%fused_computation.17 | convolution fusion | flops 3629187072 | bytes 13172736 | tf_op jit(solution)/shard_map/dot_general | solution.py:53
  266.7 8.0 %convolution_convert_fusion = bf16[1152,2048]{1,0:T(8,128)(2,1)} fusion(bf16[1152,768]{1,0:T(8,128)(2,1)S(1)} %fusion.12, bf16[2048,384]{1,0:T(8,128)(2,1)} %bitcast.20, bf16[2048,384]{1,0:T(8,128)(2,1)S(1)} %bitcast.110, pred[]{:T(512)S(6)} %eq.75), kind=kOutput, calls=%fused_computation.5 | convolution fusion | flops 3640393728 | bytes 9633793 | tf_op jit(solution)/shard_map/rf,df->rd/dot_general | solution.py:55
  274.7 5.7 %all-to-all-start.1 = ((bf16[16,72,2048]{2,1,0:T(8,128)(2,1)}), bf16[16,72,2048]{2,1,0:T(8,128)(2,1)}, u32[]{:S(2)}, u32[]{:S(2)}) async-start(bf16[16,72,2048]{2,1,0:T(8,128)(2,1)} %bitcast.101), calls=%async_computation.2 | async-start | bytes 9437184 | tf_op jit(solution)/shard_map/all_to_all | solution.py:147
  280.5 0.2 fusion.46
  280.8 0.1 copy.64
  280.9 105.2 %all-to-all-done.1 = bf16[16,72,2048]{2,1,0:T(8,128)(2,1)} async-done(((bf16[16,72,2048]{2,1,0:T(8,128)(2,1)}), bf16[16,72,2048]{2,1,0:T(8,128)(2,1)}, u32[]{:S(2)}, u32[]{:S(2)}) %all-to-all-start.1) | async-done | bytes 4718624 | tf_op jit(solution)/shard_map/all_to_all | solution.py:147
  386.1 11.8 %gather_fusion = bf16[1024,2048]{1,0:T(8,128)(2,1)} fusion(bf16[1152,2048]{1,0:T(8,128)(2,1)} %bitcast.22, s32[1024]{0:T(1024)S(1)} %broadcast_clamp_fusion), kind=kCustom, calls=%fused_computation | custom fusion | bytes 8392704 | tf_op jit(solution)/shard_map/gather | solution.py:148
  397.9 6.5 %fusion = f32[128,2048]{1,0:T(8,128)S(1)} fusion(bf16[1024,2048]{1,0:T(8,128)(2,1)} %gather_fusion, f32[128,8]{1,0:T(8,128)S(1)} %copy.64), kind=kLoop, calls=%fused_computation.3 | loop fusion | flops 6029312 | bytes 5246976 | tf_op jit(solution)/shard_map/reduce_sum | solution.py:149
  404.4 0.9 add_convert_fusion
  (39 shorter events, 0.8 us)
Async XLA Ops:
  6.5 274.0 %copy-start = (bf16[2048,16]{0,1:T(8,128)(2,1)S(1)}, bf16[2048,16]{0,1:T(8,128)(2,1)}, u32[]{:S(2)}) copy-start(bf16[2048,16]{0,1:T(8,128)(2,1)} %param.23) | copy-start | bytes 196612
  6.5 3.8 copy-start.2
  6.5 9.1 %copy-start.1 = (bf16[2,256,128]{2,1,0:T(8,128)(2,1)S(1)}, bf16[2,256,128]{2,1,0:T(8,128)(2,1)}, u32[]{:S(2)}) copy-start(bf16[2,256,128]{2,1,0:T(8,128)(2,1)} %param.15) | copy-start | bytes 393220
  6.5 9.3 %copy-start.5 = (f32[128]{0:T(128)S(1)}, f32[128]{0:T(128)}, u32[]{:S(2)}) copy-start(f32[128]{0:T(128)} %param.19) | copy-start | bytes 1540
  6.5 64.2 %all-gather.4.cloned.1.call-start = ((), (), s32[]{:S(2)}) async-start(), calls=%async_computation.3 | async-start | bytes 6291456 | tf_op jit(solution)/shard_map/all_gather | solution.py:111
  7.3 23.3 %copy-start.6 = (f32[128]{0:T(128)S(1)}, f32[128]{0:T(128)}, u32[]{:S(2)}) copy-start(f32[128]{0:T(128)} %param.18) | copy-start | bytes 1540
  7.3 115.3 %reduce-scatter.2.cloned.1.call-start = ((), (), s32[]{:S(2)}) async-start(), calls=%async_computation.4 | async-start | bytes 5242880 | tf_op jit(solution)/shard_map/reduce_scatter | solution.py:122
  77.2 0.7 copy-start.4
  77.2 47.1 %copy-start.3 = (f32[2048]{0:T(1024)S(1)}, f32[2048]{0:T(1024)}, u32[]{:S(2)}) copy-start(f32[2048]{0:T(1024)} %param.22) | copy-start | bytes 24580
  133.8 6.2 %copy-start.7 = (bf16[1,2048,384]{2,1,0:T(8,128)(2,1)S(1)}, bf16[1,2048,384]{2,1,0:T(8,128)(2,1)}, u32[]{:S(2)}) copy-start(bf16[1,2048,384]{2,1,0:T(8,128)(2,1)} %param.27) | copy-start | bytes 4718596
  133.8 110.6 %all-to-all-start = ((bf16[16,72,2048]{2,1,0:T(8,128)(2,1)}), bf16[16,72,2048]{2,1,0:T(8,128)(2,1)}, u32[]{:S(2)}, u32[]{:S(2)}) async-start(bf16[16,72,2048]{2,1,0:T(8,128)(2,1)} %bitcast.100), calls=%async_computation.1 | async-start | bytes 9437184 | tf_op jit(solution)/shard_map/all_to_all | solution.py:142
  138.7 72.0 %all-gather.6.cloned.1.call-start = ((), (), s32[]{:S(2)}) async-start(), calls=%async_computation.5 | async-start | bytes 4718592 | tf_op jit(solution)/shard_map/all_gather | solution.py:115
  139.5 118.7 %all-gather.8.cloned.1.call-start = ((), (), s32[]{:S(2)}) async-start(), calls=%async_computation.6 | async-start | bytes 4718592 | tf_op jit(solution)/shard_map/all_gather | solution.py:116
  140.0 126.6 %collective-permute-start = (bf16[1,2048,384]{2,1,0:T(8,128)(2,1)S(1)}, bf16[1,2048,384]{2,1,0:T(8,128)(2,1)}, u32[]{:S(2)}, u32[]{:S(2)}) collective-permute-start(bf16[1,2048,384]{2,1,0:T(8,128)(2,1)S(1)} %copy-done.7), channel_id=1, source_target_pairs={{0,16},{16,0},{1,17},{17,1},{2,18},{18,2},{3,19},{19,3},{4,20},{20... | collective-permute-start | bytes 4718600 | tf_op jit(solution)/shard_map/ppermute | solution.py:13
  274.7 111.3 %all-to-all-start.1 = ((bf16[16,72,2048]{2,1,0:T(8,128)(2,1)}), bf16[16,72,2048]{2,1,0:T(8,128)(2,1)}, u32[]{:S(2)}, u32[]{:S(2)}) async-start(bf16[16,72,2048]{2,1,0:T(8,128)(2,1)} %bitcast.101), calls=%async_computation.2 | async-start | bytes 9437184 | tf_op jit(solution)/shard_map/all_to_all | solution.py:147
Sparse Core Ops, SparseCore 0:
  8.9 61.7 all-gather.3
  77.4 45.2 reduce-scatter.1
  141.2 69.5 all-gather.5
  212.2 45.9 all-gather.7
